TPU v7x, 32 devices: a whole 2x2x4 slice. The times are simulated.
32 devices in a mesh: parts: 2 (over x), chan: 8 (over z, y), samp: 2 (over core).
Axes of the slice: x: 2, y: 2, z: 4, core: 2. Of those that a mesh axis runs over, the one named last changes fastest.
Arguments:
- images: bfloat16 [512, 256, 784], P(('parts', 'samp'), 'chan'), parts along dimension 0, may hold values from -6 to 6
- out_grads: bfloat16 [512, 256, 196], P(('parts', 'samp'), 'chan'), parts along dimension 0, may hold values from -6 to 6
- in_signs: int32 [256, 288], P('chan'), may hold values from 0 to 1
- out_signs: int32 [256, 32], P('chan'), may hold values from 0 to 1
Outputs:
- sketch_rows: float32 [2, 256, 1024], P('samp', ('parts', 'chan')), parts along dimension 1
- r_factor: float32 [2048, 1024], P(('parts', 'chan')), parts along dimension 0
There are 2 independent parts, one for each index of `parts`. A program takes and returns all parts, laid end to end along the dimension named above; an argument that names none is the same for every part. Nothing has to cross between parts.
All inputs are finite; a program needn't handle non-finite values.
Results may differ from a plain program's by a relative error of at most 0.0003.
Values sent between devices are 32-bit elements; how exact they have to be, the bound alone decides.
No kernel may reach another device: no remote copies, remote signals or barrier semaphores. Data moves between devices by JAX's collectives and lax.ppermute only.
A program may use at most 128 MiB of HBM per device.

v0:
```python
import math
import jax
import jax.numpy as jnp
from jax import lax
from jax.sharding import PartitionSpec as P

C = 256


def project(images, out_grads, in_signs, out_signs):
    samples, channels, cells = images.shape
    side_in = math.isqrt(cells)
    side_out = side_in // 2
    picture = images.reshape(samples, channels, side_in, side_in)
    padded = jnp.pad(picture, ((0, 0), (0, 0), (1, 1), (1, 1)))
    tap_list = []
    for row_tap in range(3):
        for col_tap in range(3):
            tap_list.append(
                padded[
                    :,
                    :,
                    row_tap : row_tap + 2 * side_out - 1 : 2,
                    col_tap : col_tap + 2 * side_out - 1 : 2,
                ]
            )
    patches = jnp.stack(tap_list, axis=2).reshape(samples, channels, 9, side_out * side_out)
    width_in = in_signs.shape[1] // 9
    in_matrix = (2 * in_signs - 1).astype(jnp.bfloat16).reshape(channels, 9, width_in)
    out_matrix = (2 * out_signs - 1).astype(jnp.bfloat16)
    in_part = jnp.einsum("nctp,ctj->njp", patches, in_matrix, preferred_element_type=jnp.float32)
    out_part = jnp.einsum("ncp,cl->nlp", out_grads, out_matrix, preferred_element_type=jnp.float32)
    return (in_part, out_part)


def sketch(in_sum, out_sum, total_channels):
    in_feat = in_sum / math.sqrt(9 * total_channels)
    out_feat = out_sum / math.sqrt(total_channels)
    cells = in_sum.shape[2]
    outer = jnp.einsum(
        "nlp,njp->nlj", out_feat, in_feat, precision=lax.Precision.HIGHEST
    ) / math.sqrt(cells)
    return outer.reshape(outer.shape[0], -1)


def local(images, out_grads, in_signs, out_signs):
    samples = images.shape[0]
    in_part, out_part = project(images, out_grads, in_signs, out_signs)
    chan_count = lax.axis_size("chan")
    local_rows = samples // chan_count
    in_sum, out_sum = lax.psum((in_part, out_part), "chan")
    every = sketch(in_sum, out_sum, C)
    own = lax.dynamic_slice_in_dim(every, lax.axis_index("chan") * local_rows, local_rows, 0)
    batch_total = samples * lax.axis_size("samp")
    width = every.shape[1]
    identity_mat = jnp.eye(width, dtype=jnp.float32)
    gram_part = jnp.einsum("nk,nm->km", every, every, precision=lax.Precision.HIGHEST) / batch_total
    factor = jnp.linalg.cholesky(lax.psum(gram_part, "samp") + identity_mat).T
    rows_here = width // chan_count
    r_rows = lax.dynamic_slice_in_dim(factor, lax.axis_index("chan") * rows_here, rows_here, 0)
    return (own[None], r_rows)


def solution(mesh):
    in_specs = (
        P(("parts", "samp"), "chan", None),
        P(("parts", "samp"), "chan", None),
        P("chan", None),
        P("chan", None),
    )
    out_specs = (P("samp", ("parts", "chan"), None), P(("parts", "chan"), None))
    return jax.shard_map(local, mesh=mesh, in_specs=in_specs, out_specs=out_specs, check_vma=False)
```

profile of v0, /device:TPU:0, one launch (start us, length us, event | category | flops | bytes accessed | tf_op | source)
XLA Modules:
  0.0 630.9 jit_solution(10612608494008498298)
XLA Ops:
  7.2 4.5 copy.36
  11.7 5.5 pad_slice_fusion
  17.2 3.6 copy.37
  22.3 4.8 copy.38
  27.1 3.4 copy.39
  30.4 4.8 copy.40
  35.3 3.3 copy.41
  38.6 3.4 copy.42
  42.0 4.8 copy.43
  46.9 3.4 copy.44
  50.2 3.4 copy.45
  53.7 3.6 copy.34
  57.4 3.4 constant_dynamic-update-slice_fusion.7
  68.4 1.6 constant_dynamic-update-slice_fusion.1
  70.0 1.6 constant_dynamic-update-slice_fusion
  71.6 12.2 %convolution_bitcast_fusion = f32[128,32,196]{2,1,0:T(8,128)} fusion(bf16[32,9,32,1]{0,2,1,3:T(8,128)(2,1)S(1)} %bitcast.86, bf16[128,32,9,196]{3,1,2,0:T(8,128)(2,1)} %constant_dynamic-update-slice_fusion), kind=kOutput, calls=%fused_computation.16 | convolution fusion | flops 462422016 | bytes 17680384 | tf_op jit(solution)/shard_map/nctp,ctj->njp/dot_general | solution.py:31
  83.8 2.7 convolution_bitcast_fusion.1
  87.0 273.4 %all-reduce.8.cloned.1.call-done = (f32[128,32,196]{2,1,0:T(8,128)}, f32[128,32,196]{2,1,0:T(8,128)}) async-done(((f32[128,32,196]{2,1,0:T(8,128)}, f32[128,32,196]{2,1,0:T(8,128)}), (f32[128,32,196]{2,1,0:T(8,128)}, f32[128,32,196]{2,1,0:T(8,128)})) %all-reduce.8.cloned.1.call-update) | async-done | bytes 6422544 | tf_op jit(solution)/shard_map/psum | solution.py:51
  360.5 7.8 %fusion.6 = f32[128,32,32]{2,1,0:T(8,128)S(1)} fusion(f32[128,32,196]{2,1,0:T(8,128)} %get-tuple-element.10, f32[128,32,196]{2,1,0:T(8,128)} %get-tuple-element.11), kind=kOutput, calls=%fused_computation.21 | convolution fusion | flops 310018048 | bytes 6946816 | tf_op jit(solution)/shard_map/nlp,njp->nlj/dot_general | solution.py:40
  369.5 5.0 convolution_multiply_fusion
  375.6 26.6 %all-reduce.6.cloned.1.call-done = f32[1024,1024]{0,1:T(8,128)} async-done(((f32[1024,1024]{0,1:T(8,128)}), f32[1024,1024]{0,1:T(8,128)}) %all-reduce.6.cloned.1.call-update) | async-done | bytes 4194320 | tf_op jit(solution)/shard_map/psum | solution.py:58
  402.2 4.8 convert_add_fusion
  407.0 5.5 copy.49
  412.5 4.5 fusion
  417.0 1.9 copy-done
  418.9 11.7 %cholesky.223 = f32[128,128]{1,0:T(8,128)S(1)} custom-call(f32[128,128]{1,0:T(8,128)S(1)} %cholesky.580), custom_call_target="Cholesky" | custom-call | tf_op jit(solution)/shard_map/jit(cholesky)/cholesky | solution.py:58
  430.6 2.5 cholesky.255
  433.1 9.8 %custom-call.59 = f32[1,128,128]{1,2,0:T(8,128)S(1)} custom-call(f32[1,128,128]{2,1,0:T(8,128)S(1)} %get-tuple-element.42), custom_call_target="InvertDiagBlocksLowerTriangular" | custom-call | tf_op jit(solution)/shard_map/jit(cholesky)/cholesky | solution.py:58
  442.9 2.4 constant_dynamic-update-slice_fusion.16
  446.9 11.9 %cholesky.244 = f32[128,128]{1,0:T(8,128)S(1)} custom-call(f32[128,128]{1,0:T(8,128)S(1)} %cholesky.584), custom_call_target="Cholesky" | custom-call | tf_op jit(solution)/shard_map/jit(cholesky)/cholesky | solution.py:58
  459.4 9.8 %custom-call.60 = f32[1,128,128]{1,2,0:T(8,128)S(1)} custom-call(f32[1,128,128]{2,1,0:T(8,128)S(1)} %get-tuple-element.39), custom_call_target="InvertDiagBlocksLowerTriangular" | custom-call | tf_op jit(solution)/shard_map/jit(cholesky)/cholesky | solution.py:58
  470.5 2.1 convolution_subtract_fusion.1
  472.6 11.7 %cholesky.468 = f32[128,128]{1,0:T(8,128)S(1)} custom-call(f32[128,128]{1,0:T(8,128)S(1)} %cholesky.589), custom_call_target="Cholesky" | custom-call | tf_op jit(solution)/shard_map/jit(cholesky)/cholesky | solution.py:58
  485.6 9.8 %custom-call.61 = f32[1,128,128]{1,2,0:T(8,128)S(1)} custom-call(f32[1,128,128]{2,1,0:T(8,128)S(1)} %get-tuple-element.36), custom_call_target="InvertDiagBlocksLowerTriangular" | custom-call | tf_op jit(solution)/shard_map/jit(cholesky)/cholesky | solution.py:58
  496.5 2.3 convolution_subtract_fusion.2
  498.9 12.1 %cholesky.487 = f32[128,128]{1,0:T(8,128)S(1)} custom-call(f32[128,128]{1,0:T(8,128)S(1)} %cholesky.594), custom_call_target="Cholesky" | custom-call | tf_op jit(solution)/shard_map/jit(cholesky)/cholesky | solution.py:58
  512.3 9.8 %custom-call.62 = f32[1,128,128]{1,2,0:T(8,128)S(1)} custom-call(f32[1,128,128]{2,1,0:T(8,128)S(1)} %get-tuple-element.33), custom_call_target="InvertDiagBlocksLowerTriangular" | custom-call | tf_op jit(solution)/shard_map/jit(cholesky)/cholesky | solution.py:58
  523.2 2.3 convolution_subtract_fusion.3
  525.6 11.7 %cholesky.506 = f32[128,128]{1,0:T(8,128)S(1)} custom-call(f32[128,128]{1,0:T(8,128)S(1)} %cholesky.599), custom_call_target="Cholesky" | custom-call | tf_op jit(solution)/shard_map/jit(cholesky)/cholesky | solution.py:58
  538.6 9.9 %custom-call.63 = f32[1,128,128]{1,2,0:T(8,128)S(1)} custom-call(f32[1,128,128]{2,1,0:T(8,128)S(1)} %get-tuple-element.30), custom_call_target="InvertDiagBlocksLowerTriangular" | custom-call | tf_op jit(solution)/shard_map/jit(cholesky)/cholesky | solution.py:58
  549.5 2.3 convolution_subtract_fusion.4
  551.8 11.7 %cholesky.526 = f32[128,128]{1,0:T(8,128)S(1)} custom-call(f32[128,128]{1,0:T(8,128)S(1)} %cholesky.604), custom_call_target="Cholesky" | custom-call | tf_op jit(solution)/shard_map/jit(cholesky)/cholesky | solution.py:58
  564.8 9.8 %custom-call.64 = f32[1,128,128]{1,2,0:T(8,128)S(1)} custom-call(f32[1,128,128]{2,1,0:T(8,128)S(1)} %get-tuple-element.27), custom_call_target="InvertDiagBlocksLowerTriangular" | custom-call | tf_op jit(solution)/shard_map/jit(cholesky)/cholesky | solution.py:58
  575.6 2.0 convolution_subtract_fusion.5
  577.6 11.9 %cholesky.546 = f32[128,128]{1,0:T(8,128)S(1)} custom-call(f32[128,128]{1,0:T(8,128)S(1)} %cholesky.609), custom_call_target="Cholesky" | custom-call | tf_op jit(solution)/shard_map/jit(cholesky)/cholesky | solution.py:58
  590.8 9.8 %custom-call.65 = f32[1,128,128]{1,2,0:T(8,128)S(1)} custom-call(f32[1,128,128]{2,1,0:T(8,128)S(1)} %get-tuple-element.24), custom_call_target="InvertDiagBlocksLowerTriangular" | custom-call | tf_op jit(solution)/shard_map/jit(cholesky)/cholesky | solution.py:58
  601.4 1.8 convolution_subtract_fusion.6
  603.2 11.7 %cholesky.564 = f32[128,128]{1,0:T(8,128)S(1)} custom-call(f32[128,128]{1,0:T(8,128)S(1)} %convolution_subtract_fusion.6), custom_call_target="Cholesky" | custom-call | tf_op jit(solution)/shard_map/jit(cholesky)/cholesky | solution.py:58
  (75 shorter events, 31.3 us)
Async XLA Ops:
  7.2 353.3 %all-reduce.8.cloned.1.call-start = ((), (), s32[]{:S(2)}) async-start(), calls=%async_computation.1 | async-start | bytes 16777216 | tf_op jit(solution)/shard_map/psum | solution.py:51
  22.3 4.8 copy-start.12
  27.1 8.2 %copy-start.11 = (bf16[128,32,14,14]{0,1,3,2:T(8,128)(2,1)S(1)}, bf16[128,32,14,14]{0,1,3,2:T(8,128)(2,1)}, u32[]{:S(2)}) copy-start(bf16[128,32,14,14]{0,1,3,2:T(8,128)(2,1)} %get-tuple-element.16) | copy-start | bytes 4816900
  30.4 8.2 %copy-start.10 = (bf16[128,32,14,14]{0,1,3,2:T(8,128)(2,1)S(1)}, bf16[128,32,14,14]{0,1,3,2:T(8,128)(2,1)}, u32[]{:S(2)}) copy-start(bf16[128,32,14,14]{0,1,3,2:T(8,128)(2,1)} %get-tuple-element.17) | copy-start | bytes 4816900
  38.6 8.2 %copy-start.9 = (bf16[128,32,14,14]{0,1,3,2:T(8,128)(2,1)S(1)}, bf16[128,32,14,14]{0,1,3,2:T(8,128)(2,1)}, u32[]{:S(2)}) copy-start(bf16[128,32,14,14]{0,1,3,2:T(8,128)(2,1)} %get-tuple-element.19) | copy-start | bytes 4816900
  42.0 8.2 %copy-start.8 = (bf16[128,32,14,14]{0,1,3,2:T(8,128)(2,1)S(1)}, bf16[128,32,14,14]{0,1,3,2:T(8,128)(2,1)}, u32[]{:S(2)}) copy-start(bf16[128,32,14,14]{0,1,3,2:T(8,128)(2,1)} %get-tuple-element.12) | copy-start | bytes 4816900
  46.9 6.7 %copy-start.13 = (s32[32,288]{1,0:T(8,128)S(1)}, s32[32,288]{1,0:T(8,128)}, u32[]{:S(2)}) copy-start(s32[32,288]{1,0:T(8,128)} %param.6) | copy-start | bytes 110596
  57.3 3.4 copy-start.7
  57.4 4.9 copy-start.6
  60.8 3.1 copy-start.5
  62.3 3.1 copy-start.4
  63.8 3.1 copy-start.3
  65.4 3.1 copy-start.1
  66.9 3.1 copy-start.2
  71.6 12.2 %copy-start.14 = (s32[32,32]{1,0:T(8,128)S(1)}, s32[32,32]{1,0:T(8,128)}, u32[]{:S(2)}) copy-start(s32[32,32]{1,0:T(8,128)} %param.7) | copy-start | bytes 12292
  86.5 315.6 %all-reduce.6.cloned.1.call-start = ((), (), s32[]{:S(2)}) async-start(), calls=%async_computation | async-start | bytes 8388608 | tf_op jit(solution)/shard_map/psum | solution.py:58
  416.9 1.9 copy-start
Sparse Core Ops, SparseCore 0:
  86.7 273.7 all-reduce.7
  374.7 27.4 all-reduce.5
where the time goes:
time: 641 us; the launch traced here: 631 us
  waiting for transfers between devices  300 us (47%)
  other arithmetic  183 us (29%)
  local copies, waits for them, and re-layouts  77.6 us (12%)
  matrix products  50.8 us (8%)
  between operations  19.4 us (3%)
    psum x1, waiting for transfers between devices, local(): in_sum, out_sum = lax.psum((in_part, out_part), 'chan')  273 us
    another operation x30, other arithmetic, local(): factor = jnp.linalg.cholesky(lax.psum(gram_part, 'samp') + identity_mat).T  172 us
    another operation x10, local copies, waits for them, and re-layouts, project(): jnp.stack(tap_list, axis=2)  36.4 us
    psum x1, waiting for transfers between devices, local(): factor = jnp.linalg.cholesky(lax.psum(gram_part, 'samp') + identity_mat).T  26.6 us
    unnamed x41, local copies, waits for them, and re-layouts  25.2 us
    another operation x14, matrix products, local(): factor = jnp.linalg.cholesky(lax.psum(gram_part, 'samp') + identity_mat).T  23.1 us
  transfers between devices with their start and end apart: 2, of which 2 were waited for; matrix products, arithmetic and copies ran while one was open for 0% of the time, Pallas kernels for 0%

commit v1 on v0

--- a/solution.py
+++ b/solution.py
@@ -55,7 +55,11 @@
     width = every.shape[1]
     identity_mat = jnp.eye(width, dtype=jnp.float32)
     gram_part = jnp.einsum("nk,nm->km", every, every, precision=lax.Precision.HIGHEST) / batch_total
-    factor = jnp.linalg.cholesky(lax.psum(gram_part, "samp") + identity_mat).T
+
+    def obtain_stacks_all_over_axis(vector, chip_axis):
+        return jnp.sum(lax.all_gather(vector, chip_axis), axis=0)
+
+    factor = jnp.linalg.cholesky(obtain_stacks_all_over_axis(gram_part, "samp") + identity_mat).T
     rows_here = width // chan_count
     r_rows = lax.dynamic_slice_in_dim(factor, lax.axis_index("chan") * rows_here, rows_here, 0)
     return (own[None], r_rows)

time: 641 us -> 635 us (level)
  waiting for transfers between devices: 300 us -> 291 us
    psum x1 -> x0, waiting for transfers between devices: 26.6 us -> none  [local(): factor = jnp.linalg.cholesky(lax.psum(gram_part, 'samp') + identity_mat).T]
    all_gather x0 -> x1, waiting for transfers between devices: none -> 18 us  [obtain_stacks_all_over_axis(): return jnp.sum(lax.all_gather(vector, chip_axis), axis=0)]
    reduce_sum x0 -> x1, other arithmetic: none -> 6.68 us  [obtain_stacks_all_over_axis(): return jnp.sum(lax.all_gather(vector, chip_axis), axis=0)]
where the time goes in v1:
time: 635 us; the launch traced here: 624 us
  waiting for transfers between devices  291 us (46%)
  other arithmetic  185 us (29%)
  local copies, waits for them, and re-layouts  77.6 us (12%)
  matrix products  50.7 us (8%)
  between operations  19.4 us (3%)
    psum x1, waiting for transfers between devices, local(): in_sum, out_sum = lax.psum((in_part, out_part), 'chan')  273 us
    another operation x30, other arithmetic, local(): jnp.linalg.cholesky(obtain_stacks_all_over_axis(gram_part, 'samp') + iden...  172 us
    another operation x10, local copies, waits for them, and re-layouts, project(): jnp.stack(tap_list, axis=2)  36.4 us
    unnamed x41, local copies, waits for them, and re-layouts  25.2 us
    another operation x14, matrix products, local(): jnp.linalg.cholesky(obtain_stacks_all_over_axis(gram_part, 'samp') + iden...  23.1 us
    all_gather x1, waiting for transfers between devices, obtain_stacks_all_over_axis(): return jnp.sum(lax.all_gather(vector, chip_axis), axis=0)  18 us
  transfers between devices with their start and end apart: 2, of which 2 were waited for; matrix products, arithmetic and copies ran while one was open for 0% of the time, Pallas kernels for 0%

profile of v1, /device:TPU:0, one launch (start us, length us, event | category | flops | bytes accessed | tf_op | source)
XLA Modules:
  0.0 624.2 jit_solution(8908478942788284648)
XLA Ops:
  7.2 4.5 copy.50
  11.7 5.5 pad_slice_fusion
  17.2 3.6 copy.51
  22.3 4.8 copy.52
  27.1 3.4 copy.53
  30.4 4.8 copy.54
  35.3 3.3 copy.55
  38.6 3.4 copy.56
  42.0 4.8 copy.57
  46.9 3.4 copy.58
  50.2 3.4 copy.59
  53.7 3.6 copy.48
  57.4 3.4 constant_dynamic-update-slice_fusion.7
  68.4 1.6 constant_dynamic-update-slice_fusion.1
  70.0 1.6 constant_dynamic-update-slice_fusion
  71.6 12.2 %convolution_bitcast_fusion = f32[128,32,196]{2,1,0:T(8,128)} fusion(bf16[32,9,32,1]{0,2,1,3:T(8,128)(2,1)S(1)} %bitcast.90, bf16[128,32,9,196]{3,1,2,0:T(8,128)(2,1)} %constant_dynamic-update-slice_fusion), kind=kOutput, calls=%fused_computation.17 | convolution fusion | flops 462422016 | bytes 17680384 | tf_op jit(solution)/shard_map/nctp,ctj->njp/dot_general | solution.py:31
  83.8 2.7 convolution_bitcast_fusion.1
  87.0 273.4 %all-reduce.5.cloned.1.call-done = (f32[128,32,196]{2,1,0:T(8,128)}, f32[128,32,196]{2,1,0:T(8,128)}) async-done(((f32[128,32,196]{2,1,0:T(8,128)}, f32[128,32,196]{2,1,0:T(8,128)}), (f32[128,32,196]{2,1,0:T(8,128)}, f32[128,32,196]{2,1,0:T(8,128)})) %all-reduce.5.cloned.1.call-update) | async-done | bytes 6422544 | tf_op jit(solution)/shard_map/psum | solution.py:51
  360.5 7.8 %fusion.7 = f32[128,32,32]{2,1,0:T(8,128)S(1)} fusion(f32[128,32,196]{2,1,0:T(8,128)} %get-tuple-element.12, f32[128,32,196]{2,1,0:T(8,128)} %get-tuple-element.13), kind=kOutput, calls=%fused_computation.22 | convolution fusion | flops 310018048 | bytes 6946816 | tf_op jit(solution)/shard_map/nlp,njp->nlj/dot_general | solution.py:40
  369.5 5.0 convolution_multiply_fusion
  375.5 18.0 %all-gather.3.cloned.1.call-done = f32[2048,1024]{1,0:T(8,128)} async-done(((f32[1024,1024]{1,0:T(8,128)}), f32[2048,1024]{1,0:T(8,128)}) %all-gather.3.cloned.1.call-update) | async-done | bytes 8388624 | tf_op jit(solution)/shard_map/all_gather | solution.py:60
  393.5 6.7 %reduce_sum.11 = f32[1024,1024]{1,0:T(8,128)} reduce(f32[2,1024,1024]{2,1,0:T(8,128)} %bitcast.80, f32[]{:T(128)} %constant.293.clone.1), dimensions={0}, to_apply=%region_2.3 | reduce | flops 1048576 | bytes 12582916 | tf_op jit(solution)/shard_map/reduce_sum | solution.py:60
  400.2 5.5 copy.62
  405.7 4.4 fusion.1
  410.2 1.9 copy-done
  412.1 11.7 %cholesky.223 = f32[128,128]{1,0:T(8,128)S(1)} custom-call(f32[128,128]{1,0:T(8,128)S(1)} %cholesky.580), custom_call_target="Cholesky" | custom-call | tf_op jit(solution)/shard_map/jit(cholesky)/cholesky | solution.py:62
  423.8 2.5 cholesky.255
  426.4 9.8 %custom-call.59 = f32[1,128,128]{1,2,0:T(8,128)S(1)} custom-call(f32[1,128,128]{2,1,0:T(8,128)S(1)} %get-tuple-element.44), custom_call_target="InvertDiagBlocksLowerTriangular" | custom-call | tf_op jit(solution)/shard_map/jit(cholesky)/cholesky | solution.py:62
  436.2 2.4 constant_dynamic-update-slice_fusion.16
  440.1 11.9 %cholesky.244 = f32[128,128]{1,0:T(8,128)S(1)} custom-call(f32[128,128]{1,0:T(8,128)S(1)} %cholesky.584), custom_call_target="Cholesky" | custom-call | tf_op jit(solution)/shard_map/jit(cholesky)/cholesky | solution.py:62
  452.6 9.8 %custom-call.60 = f32[1,128,128]{1,2,0:T(8,128)S(1)} custom-call(f32[1,128,128]{2,1,0:T(8,128)S(1)} %get-tuple-element.41), custom_call_target="InvertDiagBlocksLowerTriangular" | custom-call | tf_op jit(solution)/shard_map/jit(cholesky)/cholesky | solution.py:62
  463.7 2.1 convolution_subtract_fusion.1
  465.8 11.7 %cholesky.468 = f32[128,128]{1,0:T(8,128)S(1)} custom-call(f32[128,128]{1,0:T(8,128)S(1)} %cholesky.589), custom_call_target="Cholesky" | custom-call | tf_op jit(solution)/shard_map/jit(cholesky)/cholesky | solution.py:62
  478.8 9.8 %custom-call.61 = f32[1,128,128]{1,2,0:T(8,128)S(1)} custom-call(f32[1,128,128]{2,1,0:T(8,128)S(1)} %get-tuple-element.38), custom_call_target="InvertDiagBlocksLowerTriangular" | custom-call | tf_op jit(solution)/shard_map/jit(cholesky)/cholesky | solution.py:62
  489.8 2.3 convolution_subtract_fusion.2
  492.1 12.1 %cholesky.487 = f32[128,128]{1,0:T(8,128)S(1)} custom-call(f32[128,128]{1,0:T(8,128)S(1)} %cholesky.594), custom_call_target="Cholesky" | custom-call | tf_op jit(solution)/shard_map/jit(cholesky)/cholesky | solution.py:62
  505.5 9.8 %custom-call.62 = f32[1,128,128]{1,2,0:T(8,128)S(1)} custom-call(f32[1,128,128]{2,1,0:T(8,128)S(1)} %get-tuple-element.35), custom_call_target="InvertDiagBlocksLowerTriangular" | custom-call | tf_op jit(solution)/shard_map/jit(cholesky)/cholesky | solution.py:62
  516.4 2.3 convolution_subtract_fusion.3
  518.8 11.7 %cholesky.506 = f32[128,128]{1,0:T(8,128)S(1)} custom-call(f32[128,128]{1,0:T(8,128)S(1)} %cholesky.599), custom_call_target="Cholesky" | custom-call | tf_op jit(solution)/shard_map/jit(cholesky)/cholesky | solution.py:62
  531.8 10.0 %custom-call.63 = f32[1,128,128]{1,2,0:T(8,128)S(1)} custom-call(f32[1,128,128]{2,1,0:T(8,128)S(1)} %get-tuple-element.32), custom_call_target="InvertDiagBlocksLowerTriangular" | custom-call | tf_op jit(solution)/shard_map/jit(cholesky)/cholesky | solution.py:62
  542.8 2.3 convolution_subtract_fusion.4
  545.1 11.7 %cholesky.526 = f32[128,128]{1,0:T(8,128)S(1)} custom-call(f32[128,128]{1,0:T(8,128)S(1)} %cholesky.604), custom_call_target="Cholesky" | custom-call | tf_op jit(solution)/shard_map/jit(cholesky)/cholesky | solution.py:62
  558.1 9.8 %custom-call.64 = f32[1,128,128]{1,2,0:T(8,128)S(1)} custom-call(f32[1,128,128]{2,1,0:T(8,128)S(1)} %get-tuple-element.29), custom_call_target="InvertDiagBlocksLowerTriangular" | custom-call | tf_op jit(solution)/shard_map/jit(cholesky)/cholesky | solution.py:62
  568.8 2.0 convolution_subtract_fusion.5
  570.9 11.9 %cholesky.546 = f32[128,128]{1,0:T(8,128)S(1)} custom-call(f32[128,128]{1,0:T(8,128)S(1)} %cholesky.609), custom_call_target="Cholesky" | custom-call | tf_op jit(solution)/shard_map/jit(cholesky)/cholesky | solution.py:62
  584.0 9.8 %custom-call.65 = f32[1,128,128]{1,2,0:T(8,128)S(1)} custom-call(f32[1,128,128]{2,1,0:T(8,128)S(1)} %get-tuple-element.26), custom_call_target="InvertDiagBlocksLowerTriangular" | custom-call | tf_op jit(solution)/shard_map/jit(cholesky)/cholesky | solution.py:62
  594.6 1.8 convolution_subtract_fusion.6
  596.4 11.7 %cholesky.564 = f32[128,128]{1,0:T(8,128)S(1)} custom-call(f32[128,128]{1,0:T(8,128)S(1)} %convolution_subtract_fusion.6), custom_call_target="Cholesky" | custom-call | tf_op jit(solution)/shard_map/jit(cholesky)/cholesky | solution.py:62
  (75 shorter events, 31.3 us)
Async XLA Ops:
  7.2 353.3 %all-reduce.5.cloned.1.call-start = ((), (), s32[]{:S(2)}) async-start(), calls=%async_computation.1 | async-start | bytes 16777216 | tf_op jit(solution)/shard_map/psum | solution.py:51
  22.3 4.8 copy-start.12
  27.1 8.2 %copy-start.11 = (bf16[128,32,14,14]{0,1,3,2:T(8,128)(2,1)S(1)}, bf16[128,32,14,14]{0,1,3,2:T(8,128)(2,1)}, u32[]{:S(2)}) copy-start(bf16[128,32,14,14]{0,1,3,2:T(8,128)(2,1)} %get-tuple-element.18) | copy-start | bytes 4816900
  30.4 8.2 %copy-start.10 = (bf16[128,32,14,14]{0,1,3,2:T(8,128)(2,1)S(1)}, bf16[128,32,14,14]{0,1,3,2:T(8,128)(2,1)}, u32[]{:S(2)}) copy-start(bf16[128,32,14,14]{0,1,3,2:T(8,128)(2,1)} %get-tuple-element.19) | copy-start | bytes 4816900
  38.6 8.2 %copy-start.9 = (bf16[128,32,14,14]{0,1,3,2:T(8,128)(2,1)S(1)}, bf16[128,32,14,14]{0,1,3,2:T(8,128)(2,1)}, u32[]{:S(2)}) copy-start(bf16[128,32,14,14]{0,1,3,2:T(8,128)(2,1)} %get-tuple-element.21) | copy-start | bytes 4816900
  42.0 8.2 %copy-start.8 = (bf16[128,32,14,14]{0,1,3,2:T(8,128)(2,1)S(1)}, bf16[128,32,14,14]{0,1,3,2:T(8,128)(2,1)}, u32[]{:S(2)}) copy-start(bf16[128,32,14,14]{0,1,3,2:T(8,128)(2,1)} %get-tuple-element.14) | copy-start | bytes 4816900
  46.9 6.7 %copy-start.13 = (s32[32,288]{1,0:T(8,128)S(1)}, s32[32,288]{1,0:T(8,128)}, u32[]{:S(2)}) copy-start(s32[32,288]{1,0:T(8,128)} %param.6) | copy-start | bytes 110596
  57.3 3.4 copy-start.7
  57.4 4.9 copy-start.6
  60.8 3.1 copy-start.5
  62.3 3.1 copy-start.4
  63.8 3.1 copy-start.3
  65.4 3.1 copy-start.1
  66.9 3.1 copy-start.2
  71.6 12.2 %copy-start.14 = (s32[32,32]{1,0:T(8,128)S(1)}, s32[32,32]{1,0:T(8,128)}, u32[]{:S(2)}) copy-start(s32[32,32]{1,0:T(8,128)} %param.7) | copy-start | bytes 12292
  86.5 307.0 %all-gather.3.cloned.1.call-start = ((), (), s32[]{:S(2)}) async-start(), calls=%async_computation | async-start | bytes 12582912 | tf_op jit(solution)/shard_map/all_gather | solution.py:60
  410.2 1.9 copy-start
Sparse Core Ops, SparseCore 0:
  86.7 273.7 all-reduce.4
  374.6 18.8 all-gather.2
